TPU v7x, 32 devices: a whole 2x2x4 slice. The times are simulated.
32 devices in a mesh: groups: 2 (over y), gx: 4 (over z), gy: 4 (over x, core).
Axes of the slice: x: 2, y: 2, z: 4, core: 2. Of those that a mesh axis runs over, the one named last changes fastest.
Arguments:
- tokens: bfloat16 [40, 8192], P(('groups', 'gx'), 'gy'), parts along dimension 0, may hold values from -180 to 180, as said below
- norm_gain: float32 [8192], P('gy'), may hold values from 0.1 to 1.9
- w_gate: bfloat16 [8192, 24576], P('gy', 'gx'), may hold values from -0.0625 to 0.0625
- w_up: bfloat16 [8192, 24576], P('gy', 'gx'), may hold values from -0.0625 to 0.0625
- w_down: bfloat16 [24576, 8192], P('gx', 'gy'), may hold values from -0.0390625 to 0.0390625
Outputs:
- mixed: bfloat16 [40, 8192], P(('groups', 'gx'), 'gy'), parts along dimension 0
There are 2 independent parts, one for each index of `groups`. A program takes and returns all parts, laid end to end along the dimension named above; an argument that names none is the same for every part. Nothing has to cross between parts.
Inputs may be any that keep to these rules, and one draw needn't show every extreme that they name: tokens are real-valued activations of order one to some tens.
All inputs are finite; a program needn't handle non-finite values.
Results may differ from a plain program's by a relative error of at most 0.0064.
Values may be sent and summed in bfloat16 or wider, within the bound.
No kernel may reach another device: no remote copies, remote signals or barrier semaphores. Data moves between devices by JAX's collectives and lax.ppermute only.
A program may use at most 192 MiB of HBM per device.

v0:
```python
import jax
import jax.numpy as jnp
from jax import lax
from jax.sharding import PartitionSpec as P

D = 8192
epsilon = 1e-06


def activate(both, width):
    gate = both[:, :width]
    up_part = both[:, width:]
    return (jax.nn.silu(gate) * up_part).astype(jnp.bfloat16)


def local(tokens, norm_gain, w_gate, w_up, w_down):
    values = tokens.astype(jnp.float32)
    local_sq = jnp.sum(values * values, axis=1)
    total_sq = lax.psum(local_sq, "gy")
    inverse = lax.rsqrt(total_sq / D + epsilon)
    normed = (values * inverse[:, None] * norm_gain[None, :]).astype(jnp.bfloat16)
    width = w_gate.shape[1]
    piece = lax.all_gather(normed, "gx", axis=0, tiled=True)
    gate_part = jnp.dot(piece, w_gate, preferred_element_type=jnp.float32)
    up_part = jnp.dot(piece, w_up, preferred_element_type=jnp.float32)
    partial_value = jnp.concatenate([gate_part, up_part], axis=1)
    summed = lax.psum(partial_value, "gy")
    hidden = activate(summed, width)
    result = lax.psum_scatter(
        jnp.dot(hidden, w_down, preferred_element_type=jnp.float32),
        "gx",
        scatter_dimension=0,
        tiled=True,
    )
    return result.astype(jnp.bfloat16)


def solution(mesh):
    in_specs = (P(("groups", "gx"), "gy"), P("gy"), P("gy", "gx"), P("gy", "gx"), P("gx", "gy"))
    out_specs = P(("groups", "gx"), "gy")
    return jax.shard_map(local, mesh=mesh, in_specs=in_specs, out_specs=out_specs, check_vma=False)
```

profile of v0, /device:TPU:0, one launch (start us, length us, event | category | flops | bytes accessed | tf_op | source)
XLA Modules:
  0.0 128.5 jit_solution(15527987693795817400)
XLA Ops:
  6.5 0.0 all-reduce.4.cloned.1.call-start
  6.5 0.9 fusion.5
  7.4 8.3 %psum.14 = f32[5]{0:T(128)S(1)} all-reduce(f32[5]{0:T(128)S(1)} %fusion.5), channel_id=1, replica_groups=mesh['groups'=2,'gx'=4,'gy'=4] {'gy'}, use_global_device_ids=true, to_apply=%region_1.0 | all-reduce | flops 5 | bytes 40 | tf_op jit(solution)/shard_map/psum | solution.py:19
  15.8 0.8 fusion.8
  16.6 13.6 %all-gather = bf16[4,5,2048]{2,1,0:T(8,128)(2,1)S(1)} all-gather(bf16[1,5,2048]{2,1,0:T(8,128)(2,1)S(1)} %fusion.8), channel_id=1, replica_groups=mesh['groups'=2,'gx'=4,'gy'=4] {'gx'}, dimensions={0}, use_global_device_ids=true | all-gather | bytes 102400 | tf_op jit(solution)/shard_map/all_gather | solution.py:23
  30.3 9.9 %fusion.10 = f32[20,6144]{1,0:T(8,128)S(1)} fusion(bf16[20,2048]{1,0:T(8,128)(2,1)S(1)} %reshape.3, bf16[2048,6144]{1,0:T(8,128)(2,1)} %param.7), kind=kOutput, calls=%fused_computation.14 | convolution fusion | flops 503316480 | bytes 25739264 | tf_op jit(solution)/shard_map/dot_general | solution.py:24
  40.2 9.9 %fusion.11 = f32[20,6144]{1,0:T(8,128)S(1)} fusion(bf16[20,2048]{1,0:T(8,128)(2,1)S(1)} %reshape.3, bf16[2048,6144]{1,0:T(8,128)(2,1)} %param.8), kind=kOutput, calls=%fused_computation.15 | convolution fusion | flops 503316480 | bytes 25739264 | tf_op jit(solution)/shard_map/dot_general | solution.py:25
  50.1 0.0 copy-start
  50.1 1.1 pad_maximum_fusion
  51.2 0.0 all-reduce.4.cloned.1.call-update
  51.2 37.8 %all-reduce.4.cloned.1.call-done = f32[20,12288]{1,0:T(8,128)} async-done(((f32[20,12288]{1,0:T(8,128)}), f32[20,12288]{1,0:T(8,128)}) %all-reduce.4.cloned.1.call-update) | async-done | bytes 983056 | tf_op jit(solution)/shard_map/psum | solution.py:27
  89.0 10.2 %fusion.2 = f32[20,2048]{1,0:T(8,128)S(1)} fusion(bf16[6144,2048]{1,0:T(8,128)(2,1)} %param.9, f32[20,12288]{1,0:T(8,128)} %all-reduce.4.cloned.1.call-done), kind=kOutput, calls=%fused_computation.3 | convolution fusion | flops 504053760 | bytes 26312704 | tf_op jit(solution)/shard_map/dot_general | solution.py:30
  99.3 14.6 %fusion = f32[8,2048]{1,0:T(8,128)S(1)} fusion(f32[20,2048]{1,0:T(8,128)S(1)} %fusion.2), kind=kCustom, calls=%all-reduce-scatter | all-reduce-scatter fusion | flops 65537 | bytes 229888
  113.9 2.2 %collective-permute-start = (bf16[8,2048]{1,0:T(8,128)(2,1)S(1)}, bf16[8,2048]{1,0:T(8,128)(2,1)S(1)}, u32[]{:S(2)}, u32[]{:S(2)}) collective-permute-start(bf16[8,2048]{1,0:T(8,128)(2,1)S(1)} %convert), channel_id=1, source_target_pairs={{0,4},{4,8},{8,12},{1,5},{5,9},{9,13},{2,6},{6,10},{10,14},{3,7},{... | collective-permute-start | bytes 98312
  116.2 3.2 %collective-permute-start.1 = (bf16[1,2048]{1,0:T(2,128)(2,1)S(1)}, bf16[1,2048]{1,0:T(2,128)(2,1)S(1)}, u32[]{:S(2)}, u32[]{:S(2)}) collective-permute-start(bf16[1,2048]{1,0:T(2,128)(2,1)S(1)} %slice.10), channel_id=1, source_target_pairs={{0,8},{4,12},{1,9},{5,13},{2,10},{6,14},{3,11},{7,15},{16,24},{20,... | collective-permute-start | bytes 12296
  119.4 0.0 copy-done
  119.4 0.6 dynamic-slice.4
  120.6 0.1 collective-permute-done.1
  120.7 0.0 collective-permute-done
  120.7 0.3 concatenate.4
  121.0 0.6 dynamic-slice_convert_fusion
  (4 shorter events, 0.1 us)
Async XLA Ops:
  6.5 82.5 %all-reduce.4.cloned.1.call-start = ((), (), s32[]{:S(2)}) async-start(), calls=%async_computation | async-start | bytes 2359296 | tf_op jit(solution)/shard_map/psum | solution.py:27
  50.1 69.3 %copy-start = (u32[32]{0:T(128)S(1)}, u32[32]{0:T(128)}, u32[]{:S(2)}) copy-start(u32[32]{0:T(128)} %constant.13) | copy-start | bytes 388
  113.9 6.8 %collective-permute-start = (bf16[8,2048]{1,0:T(8,128)(2,1)S(1)}, bf16[8,2048]{1,0:T(8,128)(2,1)S(1)}, u32[]{:S(2)}, u32[]{:S(2)}) collective-permute-start(bf16[8,2048]{1,0:T(8,128)(2,1)S(1)} %convert), channel_id=1, source_target_pairs={{0,4},{4,8},{8,12},{1,5},{5,9},{9,13},{2,6},{6,10},{10,14},{3,7},{... | collective-permute-start | bytes 98312
  116.2 4.5 %collective-permute-start.1 = (bf16[1,2048]{1,0:T(2,128)(2,1)S(1)}, bf16[1,2048]{1,0:T(2,128)(2,1)S(1)}, u32[]{:S(2)}, u32[]{:S(2)}) collective-permute-start(bf16[1,2048]{1,0:T(2,128)(2,1)S(1)} %slice.10), channel_id=1, source_target_pairs={{0,8},{4,12},{1,9},{5,13},{2,10},{6,14},{3,11},{7,15},{16,24},{20,... | collective-permute-start | bytes 12296
Sparse Core Ops, SparseCore 0:
  51.4 37.6 all-reduce.3
where the time goes:
time: 129 us
  waiting for transfers between devices  37.9 us (29%)
  blocking collectives  36.6 us (28%)
  matrix products  30 us (23%)
  between operations  14.1 us (11%)
  starting transfers between devices  5.42 us (4%)
  other arithmetic  2.87 us (2%)
  local copies, waits for them, and re-layouts  1.57 us (1%)
    psum x1, waiting for transfers between devices, local(): summed = lax.psum(partial_value, 'gy')  37.8 us
    unnamed x1, blocking collectives  14.6 us
    all_gather x1, blocking collectives, local(): piece = lax.all_gather(normed, 'gx', axis=0, tiled=True)  13.6 us
    dot_general x1, matrix products, local(): jnp.dot(hidden, w_down, preferred_element_type=jnp.float32)  10.2 us
    dot_general x1, matrix products, local(): up_part = jnp.dot(piece, w_up, preferred_element_type=jnp.float32)  9.91 us
    dot_general x1, matrix products, local(): gate_part = jnp.dot(piece, w_gate, preferred_element_type=jnp.float32)  9.91 us
    psum x1, blocking collectives, local(): total_sq = lax.psum(local_sq, 'gy')  8.34 us
    unnamed x2, starting transfers between devices  5.41 us
  transfers between devices with their start and end apart: 3, of which 2 were waited for; matrix products, arithmetic and copies ran while one was open for 0% of the time, Pallas kernels for 0%

commit v1 on v0

--- a/solution.py
+++ b/solution.py
@@ -20,7 +20,23 @@
     inverse = lax.rsqrt(total_sq / D + epsilon)
     normed = (values * inverse[:, None] * norm_gain[None, :]).astype(jnp.bfloat16)
     width = w_gate.shape[1]
-    piece = lax.all_gather(normed, "gx", axis=0, tiled=True)
+    n_dev_all = jax.lax.axis_size("gx")
+    pieces_in = []
+    for d in range(n_dev_all):
+        pieces_in.append((d, (d + 1) % n_dev_all))
+    vals = []
+    for d in range(n_dev_all):
+        vals.append((d, (d - 1) % n_dev_all))
+    res, main = ([normed], [normed])
+    for _ in range(n_dev_all // 2):
+        z2 = jax.lax.ppermute(res[-1], "gx", pieces_in)
+        res.append(z2)
+    for _ in range((n_dev_all - 1) // 2):
+        a_next = jax.lax.ppermute(main[-1], "gx", perm=vals)
+        main.append(a_next)
+    e_next = jnp.concatenate([*res[::-1], *main[1:]], axis=0)
+    v1 = jax.lax.axis_index("gx")
+    piece = jnp.roll(e_next, (v1 - n_dev_all // 2) * normed.shape[0], axis=0)
     gate_part = jnp.dot(piece, w_gate, preferred_element_type=jnp.float32)
     up_part = jnp.dot(piece, w_up, preferred_element_type=jnp.float32)
     partial_value = jnp.concatenate([gate_part, up_part], axis=1)

time: 129 us -> 124 us (0.961)
  blocking collectives: 36.6 us -> 23 us
  waiting for transfers between devices: 37.9 us -> 42.6 us
  starting transfers between devices: 5.42 us -> 9.29 us
    all_gather x1 -> x0, blocking collectives: 13.6 us -> none  [local(): piece = lax.all_gather(normed, 'gx', axis=0, tiled=True)]
    ppermute x0 -> x3, waiting for transfers between devices: none -> 7.7 us  [the longest x2 7.69 us: local(): z2 = jax.lax.ppermute(res[-1], 'gx', pieces_in)]
    ppermute x0 -> x3, starting transfers between devices: none -> 3.87 us  [the longest x1 2.25 us: local(): a_next = jax.lax.ppermute(main[-1], 'gx', perm=vals)]
    psum x1, waiting for transfers between devices: 37.8 us -> 34.7 us  [local(): summed = lax.psum(partial_value, 'gy')]
  transfers between devices with their start and end apart: 3 -> 6, of which waited for: 2 -> 4; matrix products, arithmetic and copies ran while one was open for 0% -> 0% of each run, Pallas kernels for 0% -> 0%
where the time goes in v1:
time: 124 us
  waiting for transfers between devices  42.6 us (34%)
  matrix products  30 us (24%)
  blocking collectives  23 us (19%)
  between operations  14.1 us (11%)
  starting transfers between devices  9.29 us (7%)
  other arithmetic  2.88 us (2%)
  local copies, waits for them, and re-layouts  2.14 us (2%)
    psum x1, waiting for transfers between devices, local(): summed = lax.psum(partial_value, 'gy')  34.7 us
    unnamed x1, blocking collectives  14.6 us
    dot_general x1, matrix products, local(): jnp.dot(hidden, w_down, preferred_element_type=jnp.float32)  10.2 us
    dot_general x1, matrix products, local(): gate_part = jnp.dot(piece, w_gate, preferred_element_type=jnp.float32)  9.91 us
    dot_general x1, matrix products, local(): up_part = jnp.dot(piece, w_up, preferred_element_type=jnp.float32)  9.9 us
    psum x1, blocking collectives, local(): total_sq = lax.psum(local_sq, 'gy')  8.34 us
    ppermute x2, waiting for transfers between devices, local(): z2 = jax.lax.ppermute(res[-1], 'gx', pieces_in)  7.69 us
    unnamed x2, starting transfers between devices  5.41 us
  transfers between devices with their start and end apart: 6, of which 4 were waited for; matrix products, arithmetic and copies ran while one was open for 0% of the time, Pallas kernels for 0%

profile of v1, /device:TPU:0, one launch (start us, length us, event | category | flops | bytes accessed | tf_op | source)
XLA Modules:
  0.0 124.0 jit_solution(17886467316569628078)
XLA Ops:
  6.5 0.0 all-reduce.4.cloned.1.call-start
  6.5 0.9 fusion.9
  7.4 8.3 %psum.14 = f32[5]{0:T(128)S(1)} all-reduce(f32[5]{0:T(128)S(1)} %fusion.9), channel_id=1, replica_groups=mesh['groups'=2,'gx'=4,'gy'=4] {'gy'}, use_global_device_ids=true, to_apply=%region_1.0 | all-reduce | flops 5 | bytes 40 | tf_op jit(solution)/shard_map/psum | solution.py:19
  15.8 0.8 fusion.11
  16.6 1.6 %collective-permute-start = (bf16[5,2048]{1,0:T(8,128)(2,1)S(1)}, bf16[5,2048]{1,0:T(8,128)(2,1)S(1)}, u32[]{:S(2)}, u32[]{:S(2)}) collective-permute-start(bf16[5,2048]{1,0:T(8,128)(2,1)S(1)} %fusion.11), channel_id=1, source_target_pairs={{0,4},{4,8},{8,12},{12,0},{1,5},{5,9},{9,13},{13,1},{2,6},{6,10},{... | collective-permute-start | bytes 61448 | tf_op jit(solution)/shard_map/ppermute | solution.py:32
  18.2 2.2 %collective-permute-start.2 = (bf16[5,2048]{1,0:T(8,128)(2,1)S(1)}, bf16[5,2048]{1,0:T(8,128)(2,1)S(1)}, u32[]{:S(2)}, u32[]{:S(2)}) collective-permute-start(bf16[5,2048]{1,0:T(8,128)(2,1)S(1)} %fusion.11), channel_id=1, source_target_pairs={{0,12},{4,0},{8,4},{12,8},{1,13},{5,1},{9,5},{13,9},{2,14},{6,2},{... | collective-permute-start | bytes 61448 | tf_op jit(solution)/shard_map/ppermute | solution.py:35
  20.5 2.0 %collective-permute-done = bf16[5,2048]{1,0:T(8,128)(2,1)S(1)} collective-permute-done((bf16[5,2048]{1,0:T(8,128)(2,1)S(1)}, bf16[5,2048]{1,0:T(8,128)(2,1)S(1)}, u32[]{:S(2)}, u32[]{:S(2)}) %collective-permute-start) | collective-permute-done | bytes 20512 | tf_op jit(solution)/shard_map/ppermute | solution.py:32
  22.5 0.0 collective-permute-start.1
  22.5 0.0 collective-permute-done.2
  22.5 5.7 %collective-permute-done.1 = bf16[5,2048]{1,0:T(8,128)(2,1)S(1)} collective-permute-done((bf16[5,2048]{1,0:T(8,128)(2,1)S(1)}, bf16[5,2048]{1,0:T(8,128)(2,1)S(1)}, u32[]{:S(2)}, u32[]{:S(2)}) %collective-permute-start.1) | collective-permute-done | bytes 20512 | tf_op jit(solution)/shard_map/ppermute | solution.py:32
  28.2 0.6 concatenate.9
  28.8 9.9 %fusion.7 = f32[20,6144]{1,0:T(8,128)S(1)} fusion(bf16[2048,6144]{1,0:T(8,128)(2,1)} %param.7, bf16[40,2048]{1,0:T(8,128)(2,1)S(1)} %concatenate.9, s32[]{:T(128)S(6)} %select_n.14), kind=kOutput, calls=%fused_computation.7 | convolution fusion | flops 503316480 | bytes 25755652 | tf_op jit(solution)/shard_map/dot_general | solution.py:40
  38.7 9.9 %fusion.5 = f32[20,6144]{1,0:T(8,128)S(1)} fusion(bf16[2048,6144]{1,0:T(8,128)(2,1)} %param.8, bf16[40,2048]{1,0:T(8,128)(2,1)S(1)} %concatenate.9, s32[]{:T(128)S(6)} %select_n.14), kind=kOutput, calls=%fused_computation.5 | convolution fusion | flops 503316480 | bytes 25755652 | tf_op jit(solution)/shard_map/dot_general | solution.py:41
  48.6 0.0 copy-start
  48.6 1.1 pad_maximum_fusion
  49.8 0.0 all-reduce.4.cloned.1.call-update
  49.8 34.7 %all-reduce.4.cloned.1.call-done = f32[20,12288]{1,0:T(8,128)} async-done(((f32[20,12288]{1,0:T(8,128)}), f32[20,12288]{1,0:T(8,128)}) %all-reduce.4.cloned.1.call-update) | async-done | bytes 983056 | tf_op jit(solution)/shard_map/psum | solution.py:43
  84.5 10.2 %fusion.2 = f32[20,2048]{1,0:T(8,128)S(1)} fusion(bf16[6144,2048]{1,0:T(8,128)(2,1)} %param.9, f32[20,12288]{1,0:T(8,128)} %all-reduce.4.cloned.1.call-done), kind=kOutput, calls=%fused_computation.3 | convolution fusion | flops 504053760 | bytes 26312704 | tf_op jit(solution)/shard_map/dot_general | solution.py:46
  94.7 14.6 %fusion = f32[8,2048]{1,0:T(8,128)S(1)} fusion(f32[20,2048]{1,0:T(8,128)S(1)} %fusion.2), kind=kCustom, calls=%all-reduce-scatter | all-reduce-scatter fusion | flops 65537 | bytes 229888
  109.4 2.2 %collective-permute-start.3 = (bf16[8,2048]{1,0:T(8,128)(2,1)S(1)}, bf16[8,2048]{1,0:T(8,128)(2,1)S(1)}, u32[]{:S(2)}, u32[]{:S(2)}) collective-permute-start(bf16[8,2048]{1,0:T(8,128)(2,1)S(1)} %convert), channel_id=1, source_target_pairs={{0,4},{4,8},{8,12},{1,5},{5,9},{9,13},{2,6},{6,10},{10,14},{3,7},{... | collective-permute-start | bytes 98312
  111.7 3.2 %collective-permute-start.4 = (bf16[1,2048]{1,0:T(2,128)(2,1)S(1)}, bf16[1,2048]{1,0:T(2,128)(2,1)S(1)}, u32[]{:S(2)}, u32[]{:S(2)}) collective-permute-start(bf16[1,2048]{1,0:T(2,128)(2,1)S(1)} %slice.10), channel_id=1, source_target_pairs={{0,8},{4,12},{1,9},{5,13},{2,10},{6,14},{3,11},{7,15},{16,24},{20,... | collective-permute-start | bytes 12296
  114.9 0.0 copy-done
  114.9 0.6 dynamic-slice.4
  116.1 0.1 collective-permute-done.4
  116.2 0.0 collective-permute-done.3
  116.2 0.3 concatenate.11
  116.5 0.6 dynamic-slice_convert_fusion
  (3 shorter events, 0.0 us)
Async XLA Ops:
  6.5 78.0 %all-reduce.4.cloned.1.call-start = ((), (), s32[]{:S(2)}) async-start(), calls=%async_computation | async-start | bytes 2359296 | tf_op jit(solution)/shard_map/psum | solution.py:43
  16.6 5.9 %collective-permute-start = (bf16[5,2048]{1,0:T(8,128)(2,1)S(1)}, bf16[5,2048]{1,0:T(8,128)(2,1)S(1)}, u32[]{:S(2)}, u32[]{:S(2)}) collective-permute-start(bf16[5,2048]{1,0:T(8,128)(2,1)S(1)} %fusion.11), channel_id=1, source_target_pairs={{0,4},{4,8},{8,12},{12,0},{1,5},{5,9},{9,13},{13,1},{2,6},{6,10},{... | collective-permute-start | bytes 61448 | tf_op jit(solution)/shard_map/ppermute | solution.py:32
  18.2 4.3 %collective-permute-start.2 = (bf16[5,2048]{1,0:T(8,128)(2,1)S(1)}, bf16[5,2048]{1,0:T(8,128)(2,1)S(1)}, u32[]{:S(2)}, u32[]{:S(2)}) collective-permute-start(bf16[5,2048]{1,0:T(8,128)(2,1)S(1)} %fusion.11), channel_id=1, source_target_pairs={{0,12},{4,0},{8,4},{12,8},{1,13},{5,1},{9,5},{13,9},{2,14},{6,2},{... | collective-permute-start | bytes 61448 | tf_op jit(solution)/shard_map/ppermute | solution.py:35
  22.5 5.7 %collective-permute-start.1 = (bf16[5,2048]{1,0:T(8,128)(2,1)S(1)}, bf16[5,2048]{1,0:T(8,128)(2,1)S(1)}, u32[]{:S(2)}, u32[]{:S(2)}) collective-permute-start(bf16[5,2048]{1,0:T(8,128)(2,1)S(1)} %collective-permute-done), channel_id=1, source_target_pairs={{0,4},{4,8},{8,12},{12,0},{1,5},{5,9},{9,13},{13,1},{2,6},{6,10},{... | collective-permute-start | bytes 61448 | tf_op jit(solution)/shard_map/ppermute | solution.py:32
  48.6 66.2 %copy-start = (u32[32]{0:T(128)S(1)}, u32[32]{0:T(128)}, u32[]{:S(2)}) copy-start(u32[32]{0:T(128)} %constant.42) | copy-start | bytes 388
  109.4 6.8 %collective-permute-start.3 = (bf16[8,2048]{1,0:T(8,128)(2,1)S(1)}, bf16[8,2048]{1,0:T(8,128)(2,1)S(1)}, u32[]{:S(2)}, u32[]{:S(2)}) collective-permute-start(bf16[8,2048]{1,0:T(8,128)(2,1)S(1)} %convert), channel_id=1, source_target_pairs={{0,4},{4,8},{8,12},{1,5},{5,9},{9,13},{2,6},{6,10},{10,14},{3,7},{... | collective-permute-start | bytes 98312
  111.7 4.5 %collective-permute-start.4 = (bf16[1,2048]{1,0:T(2,128)(2,1)S(1)}, bf16[1,2048]{1,0:T(2,128)(2,1)S(1)}, u32[]{:S(2)}, u32[]{:S(2)}) collective-permute-start(bf16[1,2048]{1,0:T(2,128)(2,1)S(1)} %slice.10), channel_id=1, source_target_pairs={{0,8},{4,12},{1,9},{5,13},{2,10},{6,14},{3,11},{7,15},{16,24},{20,... | collective-permute-start | bytes 12296
Sparse Core Ops, SparseCore 0:
  49.9 34.5 all-reduce.3
